TPU v7x, 128 devices: a whole 4x4x4 slice. The times are simulated.
128 devices in a mesh: chan: 8 (over y_hi, x), tm: 16 (over z, y_lo, core).
Axes of the slice: x: 4, y: 4 (y_hi: 2, y_lo: 2; y = y_hi * 2 + y_lo), z: 4, core: 2. Of those that a mesh axis runs over, the one named last changes fastest.
Arguments:
- traces: bfloat16 [128, 1024, 2048], P('tm', 'chan'), may hold values from -6 to 6
- live: int32 [1024], P('chan'), may hold values 0 or 1
Outputs:
- correlations: bfloat16 [1024, 128, 2048], P(('chan', 'tm'))
Inputs may be any that keep to these rules, and one draw needn't show every extreme that they name: `live`: 1 marks a usable channel, 0 a dead one.
All inputs are finite; a program needn't handle non-finite values. No bound on the sum of `live` on one device may be relied on, other than what follows from the above.
Results may differ from a plain program's by a relative error of at most 0.0076.
Values may be sent and summed in bfloat16 or wider, within the bound.
No kernel may reach another device: no remote copies, remote signals or barrier semaphores. Data moves between devices by JAX's collectives and lax.ppermute only.
A program may use at most 128 MiB of HBM per device.

v0:
```python
import math
import jax
import jax.numpy as jnp
from jax import lax
from jax.sharding import PartitionSpec as P

SMOOTH = 4


def from_behind(block, axis, distance):
    devices = range(lax.axis_size(axis))
    route = [(i - distance, i) for i in devices if i - distance in devices]
    return lax.ppermute(block, axis, route)


def column_bins(count, group_width):
    index = jnp.arange(count, dtype=jnp.int32)
    group = index // (2 * group_width)
    within = index % group_width
    is_imag = index // group_width % 2
    return (group * group_width + within, is_imag)


def forward_table(samples, bins, group_width):
    freq, is_imag = column_bins(2 * bins, group_width)
    moments = jnp.arange(samples, dtype=jnp.int32)[:, None]
    phase = (moments * freq[None, :] % samples).astype(jnp.float32) * (2.0 * math.pi / samples)
    return jnp.where(is_imag[None, :] == 1, -jnp.sin(phase), jnp.cos(phase)).astype(jnp.bfloat16)


def inverse_table(samples, bins, group_width, segments):
    freq, is_imag = column_bins(2 * bins, group_width)
    lag = jnp.arange(samples, dtype=jnp.int32) - samples // 2
    phase = jnp.mod(freq[:, None] * lag[None, :], samples).astype(jnp.float32) * (
        2.0 * math.pi / samples
    )
    weight = jnp.where(freq == 0, 1.0, 2.0).astype(jnp.float32) / math.sqrt(samples * segments)
    wave = jnp.where(is_imag[:, None] == 1, -jnp.sin(phase), jnp.cos(phase))
    return (weight[:, None] * wave).astype(jnp.bfloat16)


def whiten(spectra, groups):
    lead = spectra.shape[:-1]
    bins = spectra.shape[-1] // 2
    width = bins // groups
    split = spectra.reshape(lead + (groups, 2, width))
    real_part = split[..., 0, :].reshape(lead + (bins,))
    imag_part = split[..., 1, :].reshape(lead + (bins,))
    amplitude = jnp.sqrt(real_part * real_part + imag_part * imag_part)
    padded = jnp.pad(amplitude, [(0, 0)] * len(lead) + [(SMOOTH, SMOOTH)])
    smooth = sum((padded[..., i : i + bins] for i in range(2 * SMOOTH + 1))) / (2 * SMOOTH + 1)
    water = 0.8 * jnp.mean(amplitude, axis=-1, keepdims=True) + 1e-06
    level = jnp.maximum(smooth, water).reshape(lead + (groups, 1, width))
    return (split / level).reshape(lead + (2 * bins,)).astype(jnp.bfloat16)


def band(matrix):
    rows, width, extra = matrix.shape
    flat = matrix.reshape(rows * width, extra)
    flat = jnp.pad(flat, ((0, rows), (0, 0)))
    return flat.reshape(rows, width + 1, extra)[:, 1 : rows + 1, :]


def product(left, right):
    return jnp.einsum("sah,sbh->abh", left, right, preferred_element_type=jnp.float32)


def cross(own_white, extended, own_flags, ext_flags, half):
    own_real = own_white[..., :half]
    own_imag = own_white[..., half:]
    ext_real = extended[..., :half]
    ext_imag = extended[..., half:]
    real_sum = product(own_real, ext_real) + product(own_imag, ext_imag)
    imag_sum = product(own_imag, ext_real) - product(own_real, ext_imag)
    pair_flags = band((own_flags[:, None] * ext_flags[None, :])[:, :, None])
    both = jnp.concatenate([band(real_sum), band(imag_sum)], axis=-1)
    return (both * pair_flags).astype(jnp.bfloat16)


def transform_rows(traces_part, table, groups):
    seg_dev, rows, samples = traces_part.shape
    spectra = jnp.dot(
        traces_part.reshape(seg_dev * rows, samples), table, preferred_element_type=jnp.float32
    )
    return whiten(spectra.reshape(seg_dev, rows, table.shape[1]), groups)


def body(traces, live):
    seg_dev, block, samples = traces.shape
    bins = samples // 2
    groups = lax.axis_size("tm")
    group_width = bins // groups
    segments = seg_dev * groups
    table = forward_table(samples, bins, group_width)
    inverse = inverse_table(samples, bins, group_width, segments)
    flags = live.astype(jnp.bfloat16)
    white = transform_rows(traces, table, groups)
    own_white = lax.all_to_all(white, "tm", split_axis=2, concat_axis=0, tiled=True)
    next_white, next_flags = from_behind((own_white, flags), "chan", -1)
    extended = jnp.concatenate([own_white, next_white], axis=1)
    ext_flags = jnp.concatenate([flags, next_flags], axis=0).astype(jnp.float32)
    stack = cross(own_white, extended, flags.astype(jnp.float32), ext_flags, group_width)
    lagged = jnp.einsum(
        "rif,fl->ril",
        lax.all_to_all(stack, "tm", split_axis=0, concat_axis=2, tiled=True),
        inverse,
        preferred_element_type=jnp.float32,
    )
    return lagged.astype(jnp.bfloat16)


def solution(mesh):
    in_specs = (P("tm", "chan", None), P("chan"))
    out_specs = P(("chan", "tm"), None, None)
    return jax.shard_map(body, mesh=mesh, in_specs=in_specs, out_specs=out_specs, check_vma=False)
```

profile of v0, /device:TPU:15, one launch (start us, length us, event | category | flops | bytes accessed | tf_op | source)
XLA Modules:
  0.0 501.4 jit_solution(12452085739045821830)
XLA Ops:
  0.6 67.4 %select_convert_fusion.4 = bf16[2048,2048]{1,0:T(8,128)(2,1)S(1)} fusion(s32[2048]{0:T(1024)S(1)} %fusion.52, pred[2048]{0:T(1024)(128)(4,1)S(1)} %fusion.49), kind=kLoop, calls=%fused_computation.15.clone.clone.1 | loop fusion | flops 71303168 | bytes 8398848 | tf_op jit(solution)/shard_map/dot_general | solution.py:82
  68.0 11.0 %fusion.12 = f32[2048,1024]{0,1:T(8,128)} fusion(bf16[1024,2048]{1,0:T(8,128)(2,1)S(1)} %bitcast.77, bf16[2048,2048]{1,0:T(8,128)(2,1)S(1)} %select_convert_fusion.4), kind=kOutput, calls=%fused_computation.21 | convolution fusion | flops 8589934592 | bytes 20971520 | tf_op jit(solution)/shard_map/dot_general | solution.py:82
  79.0 9.7 %copy.20 = f32[1024,2048]{0,1:T(8,128)} copy(f32[1024,2048]{1,0:T(8,128)} %bitcast.67) | data formatting | bytes 16777216 | tf_op jit(solution)/shard_map/dot_general | solution.py:82
  88.7 5.5 %copy.39 = f32[256,8,8,128]{3,2,1,0:T(8,128)S(1)} copy(f32[256,8,8,128]{3,1,2,0:T(8,128)} %bitcast.70) | data formatting | bytes 16777216
  95.6 2.8 copy.21
  98.4 9.1 %copy.22 = f32[8,128,2048]{1,2,0:T(8,128)} copy(f32[8,128,2048]{2,1,0:T(8,128)} %bitcast.68) | data formatting | bytes 16777216 | tf_op jit(solution)/shard_map/reshape;reshape | solution.py:46
  107.5 18.4 %multiply_maximum_fusion = f32[8,128,1024]{1,2,0:T(8,128)} fusion(f32[8,128,1024]{1,2,0:T(8,128)} %bitcast.72, f32[8,128]{1,0:T(8,128)S(1)} %multiply_add_fusion), kind=kLoop, calls=%fused_computation.48 | loop fusion | flops 10485760 | bytes 8392704 | tf_op jit(solution)/shard_map/max | solution.py:53
  125.9 5.0 %fusion.14 = bf16[8,128,2048]{1,2,0:T(8,128)(2,1)} fusion(f32[8,128,2048]{1,2,0:T(8,128)S(1)} %copy-done, f32[8,128,16,64]{1,3,2,0:T(8,128)} %bitcast.73), kind=kLoop, calls=%fused_computation.26 | loop fusion | flops 4194304 | bytes 16777216 | tf_op jit(solution)/shard_map/convert_element_type | solution.py:54
  131.0 4.9 copy.23
  135.9 55.9 %all_to_all.36 = bf16[8,128,2048]{1,0,2:T(8,128)(2,1)S(1)} all-to-all(bf16[8,128,2048]{1,0,2:T(8,128)(2,1)S(1)} %copy.23), channel_id=1, replica_groups=mesh['chan'=8,'tm'=16] {'tm'}, dimensions={2} | all-to-all | bytes 8388608 | tf_op jit(solution)/shard_map/all_to_all | solution.py:98
  191.7 3.2 copy.46
  195.0 2.4 collective-permute-start
  197.4 2.3 collective-permute-start.1
  199.8 92.7 %collective-permute-done.1 = bf16[128]{0:T(256)(128)(2,1)S(1)} collective-permute-done((bf16[128]{0:T(256)(128)(2,1)S(1)}, bf16[128]{0:T(256)(128)(2,1)S(1)}, u32[]{:S(2)}, u32[]{:S(2)}) %collective-permute-start.1) | collective-permute-done | bytes 288 | tf_op jit(solution)/shard_map/ppermute | solution.py:13
  294.1 4.2 fusion.37
  298.4 7.9 %add_bitcast_fusion = f32[128,256,64]{0,1,2:T(8,128)} fusion(f32[64,256,128]{2,1,0:T(8,128)S(1)} %fusion.37, bf16[128,128,128]{1,0,2:T(8,128)(2,1)} %bitcast.64, bf16[128,128,128]{1,0,2:T(8,128)(2,1)} %collective-permute-done), kind=kOutput, calls=%fused_computation.31 | convolution fusion | flops 555745280 | bytes 27262976 | tf_op jit(solution)/shard_map/sah,sbh->abh/dot_general | solution.py:65
  306.2 9.2 %copy.40 = f32[8,8,128,256]{3,1,2,0:T(8,128)} copy(f32[8,8,128,256]{2,3,1,0:T(8,128)} %bitcast.75) | data formatting | bytes 16777216
  315.4 7.2 %pad.16 = f32[32896,64]{0,1:T(8,128)} pad(f32[32768,64]{0,1:T(8,128)} %bitcast.66, f32[]{:T(128)} %constant.116.clone.1), padding=0_128x0_0 | pad | bytes 16809988 | tf_op jit(solution)/shard_map/jit(_pad)/pad | solution.py:60
  322.6 14.2 %reshape.174 = f32[128,257,64]{1,0,2:T(8,128)} reshape(f32[32896,64]{0,1:T(8,128)} %pad.16) | data formatting | bytes 16842752 | tf_op jit(solution)/shard_map/reshape | solution.py:61
  336.8 6.5 %slice.73 = f32[128,128,64]{1,0,2:T(8,128)} slice(f32[128,257,64]{1,0,2:T(8,128)} %reshape.174), slice={[0:128], [1:129], [0:64]} | slice | bytes 8388608 | tf_op jit(solution)/shard_map/slice | solution.py:61
  343.3 4.2 fusion.39
  347.5 7.9 %subtract_bitcast_fusion = f32[128,256,64]{0,1,2:T(8,128)} fusion(f32[64,256,128]{2,1,0:T(8,128)S(1)} %fusion.39, bf16[128,128,128]{1,0,2:T(8,128)(2,1)} %bitcast.64, bf16[128,128,128]{1,0,2:T(8,128)(2,1)} %collective-permute-done), kind=kOutput, calls=%fused_computation.30 | convolution fusion | flops 555745280 | bytes 27262976 | tf_op jit(solution)/shard_map/sah,sbh->abh/dot_general | solution.py:65
  355.4 9.2 %copy.41 = f32[8,8,128,256]{3,1,2,0:T(8,128)} copy(f32[8,8,128,256]{2,3,1,0:T(8,128)} %bitcast.74) | data formatting | bytes 16777216
  364.6 7.2 %pad.17 = f32[32896,64]{0,1:T(8,128)} pad(f32[32768,64]{0,1:T(8,128)} %bitcast.65, f32[]{:T(128)} %constant.116.clone.1), padding=0_128x0_0 | pad | bytes 16809988 | tf_op jit(solution)/shard_map/jit(_pad)/pad | solution.py:60
  371.7 14.2 %reshape.176 = f32[128,257,64]{1,0,2:T(8,128)} reshape(f32[32896,64]{0,1:T(8,128)} %pad.17) | data formatting | bytes 16842752 | tf_op jit(solution)/shard_map/reshape | solution.py:61
  385.9 4.7 slice.74
  392.0 4.7 copy.31
  396.8 5.5 %all-to-all-start.1 = ((bf16[128,128,128]{1,2,0:T(8,128)(2,1)}), bf16[128,128,128]{1,2,0:T(8,128)(2,1)}, u32[]{:S(2)}, u32[]{:S(2)}) async-start(bf16[128,128,128]{1,2,0:T(8,128)(2,1)} %copy.31), calls=%async_computation.1 | async-start | bytes 8388608 | tf_op jit(solution)/shard_map/all_to_all | solution.py:105
  402.3 71.1 %fusion.72 = bf16[2048,2048,1]{1,0,2:T(8,128)(2,1)} fusion(s32[2048]{0:T(1024)S(1)} %iota_add_fusion, s32[2048]{0:T(1024)S(1)} %copy-done.4, f32[2048]{0:T(1024)S(1)} %select_multiply_fusion, pred[2048]{0:T(1024)(128)(4,1)S(1)} %copy-done.6), kind=kLoop, calls=%fused_computation.19.clone.clone.clone.clone.1 | loop fusion | flops 75497472 | bytes 8415232 | tf_op jit(solution)/shard_map/rif,fl->ril/dot_general | solution.py:103
  473.4 6.7 %copy.33 = bf16[8,128,16,128]{3,2,1,0:T(8,128)(2,1)} copy(bf16[8,128,16,128]{1,3,0,2:T(8,128)(2,1)} %bitcast.15) | data formatting | bytes 8388608 | tf_op jit(solution)/shard_map/all_to_all | solution.py:105
  480.1 7.3 %all_to_all.33 = bf16[8,128,2048]{2,1,0:T(8,128)(2,1)} reshape(bf16[8,128,16,128]{3,2,1,0:T(8,128)(2,1)} %copy.33) | data formatting | bytes 8388608 | tf_op jit(solution)/shard_map/all_to_all | solution.py:105
  487.4 13.8 %fusion.33 = bf16[8,128,2048]{2,1,0:T(8,128)(2,1)} fusion(bf16[8,128,2048]{2,1,0:T(8,128)(2,1)} %all_to_all.33, bf16[2048,2048,1]{1,0,2:T(8,128)(2,1)} %fusion.72), kind=kOutput, calls=%fused_computation.54 | convolution fusion | flops 8592031744 | bytes 16777216 | tf_op jit(solution)/shard_map/rif,fl->ril/dot_general | solution.py:103
  (34 shorter events, 5.1 us)
Async XLA Ops:
  0.0 68.0 %copy-start.7 = (bf16[8,128,2048]{2,1,0:T(8,128)(2,1)S(1)}, bf16[8,128,2048]{2,1,0:T(8,128)(2,1)}, u32[]{:S(2)}) copy-start(bf16[8,128,2048]{2,1,0:T(8,128)(2,1)} %param.2) | copy-start | bytes 12582916
  0.0 0.6 copy-start.3
  0.6 67.4 %copy-start.5 = (pred[2048]{0:T(1024)(128)(4,1)}, pred[2048]{0:T(1024)(128)(4,1)S(1)}, u32[]{:S(2)}) copy-start(pred[2048]{0:T(1024)(128)(4,1)S(1)} %fusion.49) | copy-start | bytes 6148
  107.5 18.4 %copy-start = (f32[8,128,2048]{1,2,0:T(8,128)S(1)}, f32[8,128,2048]{1,2,0:T(8,128)}, u32[]{:S(2)}) copy-start(f32[8,128,2048]{1,2,0:T(8,128)} %copy.22) | copy-start | bytes 25165828
  135.8 61.6 %copy-start.8 = (s32[128]{0:T(128)S(1)}, s32[128]{0:T(128)}, u32[]{:S(2)}) copy-start(s32[128]{0:T(128)} %param.3) | copy-start | bytes 1540
  195.0 99.2 %collective-permute-start = (bf16[128,128,128]{1,0,2:T(8,128)(2,1)}, bf16[128,128,128]{1,0,2:T(8,128)(2,1)}, u32[]{:S(2)}, u32[]{:S(2)}) collective-permute-start(bf16[128,128,128]{1,0,2:T(8,128)(2,1)} %bitcast.64), channel_id=1, source_target_pairs={{16,0},{32,16},{48,32},{64,48},{80,64},{96,80},{112,96},{17,1},{33... | collective-permute-start | bytes 12582920 | tf_op jit(solution)/shard_map/ppermute | solution.py:13
  197.4 95.1 %collective-permute-start.1 = (bf16[128]{0:T(256)(128)(2,1)S(1)}, bf16[128]{0:T(256)(128)(2,1)S(1)}, u32[]{:S(2)}, u32[]{:S(2)}) collective-permute-start(bf16[128]{0:T(256)(128)(2,1)S(1)} %get-tuple-element.8), channel_id=1, source_target_pairs={{16,0},{32,16},{48,32},{64,48},{80,64},{96,80},{112,96},{17,1},{33... | collective-permute-start | bytes 776 | tf_op jit(solution)/shard_map/ppermute | solution.py:13
  385.9 4.7 copy-start.1
  385.9 4.7 copy-start.2
  392.0 10.2 %copy-start.4 = (s32[2048]{0:T(1024)S(1)}, s32[2048]{0:T(1024)}, u32[]{:S(2)}) copy-start(s32[2048]{0:T(1024)} %copy-done.3) | copy-start | bytes 24580
  392.0 10.2 %copy-start.6 = (pred[2048]{0:T(1024)(128)(4,1)S(1)}, pred[2048]{0:T(1024)(128)(4,1)}, u32[]{:S(2)}) copy-start(pred[2048]{0:T(1024)(128)(4,1)} %copy-done.5) | copy-start | bytes 6148
  396.8 76.6 %all-to-all-start.1 = ((bf16[128,128,128]{1,2,0:T(8,128)(2,1)}), bf16[128,128,128]{1,2,0:T(8,128)(2,1)}, u32[]{:S(2)}, u32[]{:S(2)}) async-start(bf16[128,128,128]{1,2,0:T(8,128)(2,1)} %copy.31), calls=%async_computation.1 | async-start | bytes 8388608 | tf_op jit(solution)/shard_map/all_to_all | solution.py:105
where the time goes:
time: 509 us; the launch traced here: 501 us
  other arithmetic  165 us (32%)
  local copies, waits for them, and re-layouts  128 us (25%)
  waiting for transfers between devices  92.7 us (18%)
  blocking collectives  55.9 us (11%)
  matrix products  49 us (10%)
  starting transfers between devices  10.3 us (2%)
    ppermute x2, waiting for transfers between devices, from_behind(): return lax.ppermute(block, axis, route)  92.7 us
    dot_general x1, other arithmetic, body(): jnp.einsum('rif,fl->ril', lax.all_to_all(stack, 'tm', split_axis=0, conca...  71.1 us
    dot_general x1, other arithmetic, transform_rows(): jnp.dot(traces_part.reshape(seg_dev * rows, samples), table, preferred_el...  67.4 us
    all_to_all x1, blocking collectives, body(): lax.all_to_all(white, 'tm', split_axis=2, concat_axis=0, tiled=True)  55.9 us
    reshape x3, local copies, waits for them, and re-layouts, band(): return flat.reshape(rows, width + 1, extra)[:, 1:rows + 1, :]  28.7 us
    unnamed x22, local copies, waits for them, and re-layouts  24.6 us
    dot_general x4, matrix products, product(): jnp.einsum('sah,sbh->abh', left, right, preferred_element_type=jnp.float32)  24.2 us
    max x1, other arithmetic, whiten(): level = jnp.maximum(smooth, water).reshape(lead + (groups, 1, width))  18.4 us
  transfers between devices with their start and end apart: 3, of which 1 were waited for; matrix products, arithmetic and copies ran while one was open for 14% of the time, Pallas kernels for 0%

commit v1 on v0

--- a/solution.py
+++ b/solution.py
@@ -102,7 +102,10 @@
     stack = cross(own_white, extended, flags.astype(jnp.float32), ext_flags, group_width)
     lagged = jnp.einsum(
         "rif,fl->ril",
-        lax.all_to_all(stack, "tm", split_axis=0, concat_axis=2, tiled=True),
+        jnp.concatenate(
+            lax.all_to_all(jnp.stack(jnp.split(stack, lax.axis_size("tm"), axis=0)), "tm", 0, 0),
+            axis=2,
+        ),
         inverse,
         preferred_element_type=jnp.float32,
     )

time: 509 us -> 503 us (0.988)
  local copies, waits for them, and re-layouts: 128 us -> 121 us
    all_to_all x2 -> x0, local copies, waits for them, and re-layouts: 14 us -> none  [body(): lax.all_to_all(stack, 'tm', split_axis=0, concat_axis=2, tiled=True)]
    unnamed x22 -> x37, local copies, waits for them, and re-layouts: 24.6 us -> 35.7 us
  transfers between devices with their start and end apart: 3 -> 3, of which waited for: 1 -> 1; matrix products, arithmetic and copies ran while one was open for 14% -> 15% of each run, Pallas kernels for 0% -> 0%
where the time goes in v1:
time: 503 us; the launch traced here: 495 us
  other arithmetic  165 us (33%)
  local copies, waits for them, and re-layouts  121 us (24%)
  waiting for transfers between devices  92.9 us (18%)
  blocking collectives  55.9 us (11%)
  matrix products  49.2 us (10%)
  starting transfers between devices  10.6 us (2%)
    ppermute x2, waiting for transfers between devices, from_behind(): return lax.ppermute(block, axis, route)  92.9 us
    dot_general x1, other arithmetic, body(): jnp.einsum('rif,fl->ril', jnp.concatenate(lax.all_to_all(jnp.stack(jnp.sp...  71.1 us
    dot_general x1, other arithmetic, transform_rows(): jnp.dot(traces_part.reshape(seg_dev * rows, samples), table, preferred_el...  67.4 us
    all_to_all x1, blocking collectives, body(): lax.all_to_all(white, 'tm', split_axis=2, concat_axis=0, tiled=True)  55.9 us
    unnamed x37, local copies, waits for them, and re-layouts  35.7 us
    reshape x3, local copies, waits for them, and re-layouts, band(): return flat.reshape(rows, width + 1, extra)[:, 1:rows + 1, :]  28.7 us
    dot_general x4, matrix products, product(): jnp.einsum('sah,sbh->abh', left, right, preferred_element_type=jnp.float32)  24.2 us
    max x1, other arithmetic, whiten(): level = jnp.maximum(smooth, water).reshape(lead + (groups, 1, width))  18.4 us
  transfers between devices with their start and end apart: 3, of which 1 were waited for; matrix products, arithmetic and copies ran while one was open for 15% of the time, Pallas kernels for 0%

profile of v1, /device:TPU:15, one launch (start us, length us, event | category | flops | bytes accessed | tf_op | source)
XLA Modules:
  0.0 495.3 jit_solution(8928700729832364326)
XLA Ops:
  0.0 67.4 %select_convert_fusion.4 = bf16[2048,2048]{1,0:T(8,128)(2,1)S(1)} fusion(s32[2048]{0:T(1024)S(1)} %fusion.71, pred[2048]{0:T(1024)(128)(4,1)S(1)} %fusion.68), kind=kLoop, calls=%fused_computation.15.clone.clone.1 | loop fusion | flops 71303168 | bytes 8398848 | tf_op jit(solution)/shard_map/dot_general | solution.py:82
  67.5 11.0 %fusion.12 = f32[2048,1024]{0,1:T(8,128)} fusion(bf16[1024,2048]{1,0:T(8,128)(2,1)S(1)} %bitcast.137, bf16[2048,2048]{1,0:T(8,128)(2,1)S(1)} %select_convert_fusion.4), kind=kOutput, calls=%fused_computation.21 | convolution fusion | flops 8589934592 | bytes 20971520 | tf_op jit(solution)/shard_map/dot_general | solution.py:82
  78.5 9.7 %copy.36 = f32[1024,2048]{0,1:T(8,128)} copy(f32[1024,2048]{1,0:T(8,128)} %bitcast.127) | data formatting | bytes 16777216 | tf_op jit(solution)/shard_map/dot_general | solution.py:82
  88.2 5.5 %copy.56 = f32[256,8,8,128]{3,2,1,0:T(8,128)S(1)} copy(f32[256,8,8,128]{3,1,2,0:T(8,128)} %bitcast.130) | data formatting | bytes 16777216
  93.7 1.5 fusion.82
  95.2 2.8 copy.37
  97.9 9.1 %copy.38 = f32[8,128,2048]{1,2,0:T(8,128)} copy(f32[8,128,2048]{2,1,0:T(8,128)} %bitcast.128) | data formatting | bytes 16777216 | tf_op jit(solution)/shard_map/reshape;reshape | solution.py:46
  107.1 18.4 %multiply_maximum_fusion = f32[8,128,1024]{1,2,0:T(8,128)} fusion(f32[8,128,1024]{1,2,0:T(8,128)} %bitcast.132, f32[8,128]{1,0:T(8,128)S(1)} %multiply_add_fusion), kind=kLoop, calls=%fused_computation.49 | loop fusion | flops 10485760 | bytes 8392704 | tf_op jit(solution)/shard_map/max | solution.py:53
  125.4 5.0 %fusion.14 = bf16[8,128,2048]{1,2,0:T(8,128)(2,1)} fusion(f32[8,128,2048]{1,2,0:T(8,128)S(1)} %copy-done, f32[8,128,16,64]{1,3,2,0:T(8,128)} %bitcast.133), kind=kLoop, calls=%fused_computation.26 | loop fusion | flops 4194304 | bytes 16777216 | tf_op jit(solution)/shard_map/convert_element_type | solution.py:54
  130.5 4.9 copy.39
  135.4 55.9 %all_to_all.23 = bf16[8,128,2048]{1,0,2:T(8,128)(2,1)S(1)} all-to-all(bf16[8,128,2048]{1,0,2:T(8,128)(2,1)S(1)} %copy.39), channel_id=1, replica_groups=mesh['chan'=8,'tm'=16] {'tm'}, dimensions={2} | all-to-all | bytes 8388608 | tf_op jit(solution)/shard_map/all_to_all | solution.py:98
  191.3 3.2 copy.68
  194.5 2.4 collective-permute-start
  196.9 2.2 collective-permute-start.1
  199.1 92.9 %collective-permute-done.1 = bf16[128]{0:T(256)(128)(2,1)S(1)} collective-permute-done((bf16[128]{0:T(256)(128)(2,1)S(1)}, bf16[128]{0:T(256)(128)(2,1)S(1)}, u32[]{:S(2)}, u32[]{:S(2)}) %collective-permute-start.1) | collective-permute-done | bytes 288 | tf_op jit(solution)/shard_map/ppermute | solution.py:13
  293.7 4.2 fusion.40
  297.9 7.9 %add_bitcast_fusion = f32[128,256,64]{0,1,2:T(8,128)} fusion(f32[64,256,128]{2,1,0:T(8,128)S(1)} %fusion.40, bf16[128,128,128]{1,0,2:T(8,128)(2,1)} %bitcast.124, bf16[128,128,128]{1,0,2:T(8,128)(2,1)} %collective-permute-done), kind=kOutput, calls=%fused_computation.31 | convolution fusion | flops 555745280 | bytes 27262976 | tf_op jit(solution)/shard_map/sah,sbh->abh/dot_general | solution.py:65
  305.7 9.3 %copy.57 = f32[8,8,128,256]{3,1,2,0:T(8,128)} copy(f32[8,8,128,256]{2,3,1,0:T(8,128)} %bitcast.135) | data formatting | bytes 16777216
  315.1 7.2 %pad.16 = f32[32896,64]{0,1:T(8,128)} pad(f32[32768,64]{0,1:T(8,128)} %bitcast.126, f32[]{:T(128)} %constant.116.clone.1), padding=0_128x0_0 | pad | bytes 16809988 | tf_op jit(solution)/shard_map/jit(_pad)/pad | solution.py:60
  322.3 14.2 %reshape.180 = f32[128,257,64]{1,0,2:T(8,128)} reshape(f32[32896,64]{0,1:T(8,128)} %pad.16) | data formatting | bytes 16842752 | tf_op jit(solution)/shard_map/reshape | solution.py:61
  336.4 6.5 %slice.73 = f32[128,128,64]{1,0,2:T(8,128)} slice(f32[128,257,64]{1,0,2:T(8,128)} %reshape.180), slice={[0:128], [1:129], [0:64]} | slice | bytes 8388608 | tf_op jit(solution)/shard_map/slice | solution.py:61
  342.9 4.2 fusion.42
  347.2 7.9 %subtract_bitcast_fusion = f32[128,256,64]{0,1,2:T(8,128)} fusion(f32[64,256,128]{2,1,0:T(8,128)S(1)} %fusion.42, bf16[128,128,128]{1,0,2:T(8,128)(2,1)} %bitcast.124, bf16[128,128,128]{1,0,2:T(8,128)(2,1)} %collective-permute-done), kind=kOutput, calls=%fused_computation.30 | convolution fusion | flops 555745280 | bytes 27262976 | tf_op jit(solution)/shard_map/sah,sbh->abh/dot_general | solution.py:65
  355.1 9.2 %copy.58 = f32[8,8,128,256]{3,1,2,0:T(8,128)} copy(f32[8,8,128,256]{2,3,1,0:T(8,128)} %bitcast.134) | data formatting | bytes 16777216
  364.2 7.2 %pad.17 = f32[32896,64]{0,1:T(8,128)} pad(f32[32768,64]{0,1:T(8,128)} %bitcast.125, f32[]{:T(128)} %constant.116.clone.1), padding=0_128x0_0 | pad | bytes 16809988 | tf_op jit(solution)/shard_map/jit(_pad)/pad | solution.py:60
  371.4 14.2 %reshape.182 = f32[128,257,64]{1,0,2:T(8,128)} reshape(f32[32896,64]{0,1:T(8,128)} %pad.17) | data formatting | bytes 16842752 | tf_op jit(solution)/shard_map/reshape | solution.py:61
  385.6 4.7 slice.74
  390.3 1.2 fusion.13
  391.5 0.8 fusion.60
  403.9 6.0 %all-to-all-start.1 = ((bf16[16,8,128,128]{2,1,3,0:T(8,128)(2,1)}), bf16[16,8,128,128]{2,1,3,0:T(8,128)(2,1)}, u32[]{:S(2)}, u32[]{:S(2)}) async-start(bf16[16,8,128,128]{2,1,3,0:T(8,128)(2,1)} %fusion.45), calls=%async_computation.1 | async-start | bytes 8388608 | tf_op jit(solution)/shard_map/all_to_all | solution.py:106
  409.9 71.1 %fusion.90 = bf16[2048,2048,1]{1,0,2:T(8,128)(2,1)} fusion(s32[2048]{0:T(1024)S(1)} %iota_add_fusion, s32[2048]{0:T(1024)S(1)} %copy-done.4, f32[2048]{0:T(1024)S(1)} %select_multiply_fusion, pred[2048]{0:T(1024)(128)(4,1)S(1)} %copy-done.6), kind=kLoop, calls=%fused_computation.19.clone.clone.clone.clone.1 | loop fusion | flops 75497472 | bytes 8415232 | tf_op jit(solution)/shard_map/rif,fl->ril/dot_general | solution.py:103
  481.0 14.0 %fusion.34 = bf16[8,128,2048]{2,1,0:T(8,128)(2,1)} fusion(bf16[8,128,2048]{1,0,2:T(8,128)(2,1)} %bitcast.30, bf16[2048,2048,1]{1,0,2:T(8,128)(2,1)} %fusion.90), kind=kOutput, calls=%fused_computation.55 | convolution fusion | flops 8592031744 | bytes 16777216 | tf_op jit(solution)/shard_map/rif,fl->ril/dot_general | solution.py:103
  (47 shorter events, 13.3 us)
Async XLA Ops:
  0.0 67.5 %copy-start.3 = (s32[2048]{0:T(1024)}, s32[2048]{0:T(1024)S(1)}, u32[]{:S(2)}) copy-start(s32[2048]{0:T(1024)S(1)} %fusion.71) | copy-start | bytes 24580
  0.0 67.5 %copy-start.5 = (pred[2048]{0:T(1024)(128)(4,1)}, pred[2048]{0:T(1024)(128)(4,1)S(1)}, u32[]{:S(2)}) copy-start(pred[2048]{0:T(1024)(128)(4,1)S(1)} %fusion.68) | copy-start | bytes 6148
  0.0 67.5 %copy-start.7 = (bf16[8,128,2048]{2,1,0:T(8,128)(2,1)S(1)}, bf16[8,128,2048]{2,1,0:T(8,128)(2,1)}, u32[]{:S(2)}) copy-start(bf16[8,128,2048]{2,1,0:T(8,128)(2,1)} %param.2) | copy-start | bytes 12582916
  107.1 18.4 %copy-start = (f32[8,128,2048]{1,2,0:T(8,128)S(1)}, f32[8,128,2048]{1,2,0:T(8,128)}, u32[]{:S(2)}) copy-start(f32[8,128,2048]{1,2,0:T(8,128)} %copy.38) | copy-start | bytes 25165828
  191.3 5.7 %copy-start.8 = (s32[128]{0:T(128)S(1)}, s32[128]{0:T(128)}, u32[]{:S(2)}) copy-start(s32[128]{0:T(128)} %param.3) | copy-start | bytes 1540
  194.5 99.2 %collective-permute-start = (bf16[128,128,128]{1,0,2:T(8,128)(2,1)}, bf16[128,128,128]{1,0,2:T(8,128)(2,1)}, u32[]{:S(2)}, u32[]{:S(2)}) collective-permute-start(bf16[128,128,128]{1,0,2:T(8,128)(2,1)} %bitcast.124), channel_id=1, source_target_pairs={{16,0},{32,16},{48,32},{64,48},{80,64},{96,80},{112,96},{17,1},{33... | collective-permute-start | bytes 12582920 | tf_op jit(solution)/shard_map/ppermute | solution.py:13
  196.9 95.1 %collective-permute-start.1 = (bf16[128]{0:T(256)(128)(2,1)S(1)}, bf16[128]{0:T(256)(128)(2,1)S(1)}, u32[]{:S(2)}, u32[]{:S(2)}) collective-permute-start(bf16[128]{0:T(256)(128)(2,1)S(1)} %get-tuple-element.8), channel_id=1, source_target_pairs={{16,0},{32,16},{48,32},{64,48},{80,64},{96,80},{112,96},{17,1},{33... | collective-permute-start | bytes 776 | tf_op jit(solution)/shard_map/ppermute | solution.py:13
  385.6 4.7 copy-start.1
  385.6 4.7 copy-start.2
  403.9 6.0 %copy-start.4 = (s32[2048]{0:T(1024)S(1)}, s32[2048]{0:T(1024)}, u32[]{:S(2)}) copy-start(s32[2048]{0:T(1024)} %copy-done.3) | copy-start | bytes 24580
  403.9 6.0 %copy-start.6 = (pred[2048]{0:T(1024)(128)(4,1)S(1)}, pred[2048]{0:T(1024)(128)(4,1)}, u32[]{:S(2)}) copy-start(pred[2048]{0:T(1024)(128)(4,1)} %copy-done.5) | copy-start | bytes 6148
  403.9 77.1 %all-to-all-start.1 = ((bf16[16,8,128,128]{2,1,3,0:T(8,128)(2,1)}), bf16[16,8,128,128]{2,1,3,0:T(8,128)(2,1)}, u32[]{:S(2)}, u32[]{:S(2)}) async-start(bf16[16,8,128,128]{2,1,3,0:T(8,128)(2,1)} %fusion.45), calls=%async_computation.1 | async-start | bytes 8388608 | tf_op jit(solution)/shard_map/all_to_all | solution.py:106
